TPU v7x, 32 devices: a whole 2x2x4 slice. The times are simulated.
32 devices in a mesh: lon: 4 (over x, core), lat: 8 (over z, y).
Axes of the slice: x: 2, y: 2, z: 4, core: 2. Of those that a mesh axis runs over, the one named last changes fastest.
Arguments:
- prognostic: float32 [4, 16, 192, 1536], P(None, None, 'lat', 'lon'), may hold values from -6 to 6
- tracers: float32 [4, 16, 192, 1536], P(None, None, 'lat', 'lon'), may hold values from -6 to 6
- zonal_courant: float32 [16, 192, 1536], P(None, 'lat', 'lon'), may hold values from -0.45 to 0.45
- meridional_courant: float32 [16, 192, 1536], P(None, 'lat', 'lon'), may hold values from -0.45 to 0.45
- filter_band: int32 [192], P('lat'), may hold values from 96 to 768, as said below
- dep_owner: int32 [192, 2], P('lat'), may hold values from 0 to 7, as said below
- dep_row: int32 [192, 2], P('lat'), may hold values from 0 to 23
- dep_weight: float32 [192, 2], P('lat'), may hold values from 0 to 1, as said below
Outputs:
- new_prognostic: float32 [4, 16, 192, 1536], P(None, None, 'lat', 'lon')
- new_tracers: float32 [4, 16, 192, 1536], P(None, None, 'lat', 'lon')
Inputs may be any that keep to these rules, and one draw needn't show every extreme that they name: `filter_band`: rows within 24 of either pole hold values below 768; all other rows hold 768. `dep_owner`: among the 48 entries of one band, at most 12 name the same owner band, and some owner is named exactly 12 times; the owners a band names are the bands nearest to it, distance counted across either pole. `dep_weight`: Positive; the 2 weights of a row sum to 1.
All inputs are finite; a program needn't handle non-finite values.
Results may differ from a plain program's by a relative error of at most 0.00007.
Values sent between devices are 32-bit elements; how exact they have to be, the bound alone decides.
No kernel may reach another device: no remote copies, remote signals or barrier semaphores. Data moves between devices by JAX's collectives and lax.ppermute only.
A program may use at most 128 MiB of HBM per device.

v0:
```python
import math
import jax
import jax.numpy as jnp
from jax import lax
from jax.sharding import PartitionSpec as P

PRECISE = lax.Precision.HIGHEST


def padded(value, sides, width, wrap):
    for axis, dim in sides:
        size, length = (lax.axis_size(axis), value.shape[dim])
        up = [(i, (i + 1) % size) for i in range(size if wrap else size - 1)]
        down = [(j, i) for i, j in up]
        last = lax.slice_in_dim(value, length - width, length, axis=dim)
        first = lax.slice_in_dim(value, 0, width, axis=dim)
        before = lax.ppermute(last, axis, up)
        after = lax.ppermute(first, axis, down)
        value = jnp.concatenate([before, value, after], axis=dim)
    return value


def face_flux(values, speeds, axis):
    count = values.shape[axis] - 2
    left_cells = lax.slice_in_dim(values, 0, count + 1, axis=axis)
    right_cells = lax.slice_in_dim(values, 1, count + 2, axis=axis)
    courant = lax.slice_in_dim(speeds, 0, count + 1, axis=axis)
    return 0.5 * courant * (left_cells + right_cells) - 0.5 * courant * courant * (
        right_cells - left_cells
    )


def column_factors(band_rows, length):
    column = jnp.arange(length, dtype=jnp.int32)
    half_length = length // 2
    frequency = jnp.where(column <= half_length, column, column - half_length)
    single = (column == 0) | (column == half_length)
    weights = jnp.where(single, 1.0 / length, 2.0 / length).astype(jnp.float32)
    ratios = (
        band_rows.astype(jnp.float32)[:, None]
        / jnp.maximum(frequency, 1).astype(jnp.float32)[None, :]
    )
    damping = jnp.minimum(1.0, ratios * ratios)
    return (damping - 1.0) * weights[None, :]


def circle_basis(length):
    half_length = length // 2
    column = jnp.arange(length, dtype=jnp.int32)
    frequency = jnp.where(column <= half_length, column, column - half_length)
    low_count = 64
    high_count = length // low_count
    low = jnp.arange(low_count, dtype=jnp.int32)
    high = jnp.arange(high_count, dtype=jnp.int32) * low_count
    scale = 2.0 * math.pi / length
    low_angle = scale * (low[:, None] * frequency[None, :] % length).astype(jnp.float32)
    high_angle = scale * (high[:, None] * frequency[None, :] % length).astype(jnp.float32)
    low_cos, low_sin = (jnp.cos(low_angle), jnp.sin(low_angle))
    high_cos, high_sin = (jnp.cos(high_angle), jnp.sin(high_angle))
    cos_part = high_cos[:, None] * low_cos[None] - high_sin[:, None] * low_sin[None]
    sin_part = high_sin[:, None] * low_cos[None] + high_cos[:, None] * low_sin[None]
    basis = jnp.where((column <= half_length)[None, None, :], cos_part, sin_part)
    return basis.reshape(length, length)


def polar_filter(values, band_rows):
    fields, levels, rows, block_cells = values.shape
    parts = lax.axis_size("lon")
    length = block_cells * parts
    flat = values.reshape(fields * levels * rows, block_cells)
    circles = lax.all_to_all(flat, "lon", split_axis=0, concat_axis=1, tiled=True)
    basis_table = circle_basis(length)
    spectrum = jnp.dot(circles, basis_table, precision=PRECISE)
    factors = column_factors(band_rows, length)
    circle_rows = circles.shape[0]
    scaled = (spectrum.reshape(circle_rows // rows, rows, length) * factors[None]).reshape(
        circle_rows, length
    )
    change = lax.dot_general(scaled, basis_table, (((1,), (1,)), ((), ())), precision=PRECISE)
    back = lax.all_to_all(change, "lon", split_axis=1, concat_axis=0, tiled=True)
    return values + back.reshape(values.shape)


def departure_terms(tracers, dep_owner, dep_row, dep_weight):
    band_count = lax.axis_size("lat")
    row_count, link_count = dep_owner.shape
    entries = row_count * link_count
    capacity = max(2, -(-2 * entries // band_count))
    owner_ids = dep_owner.reshape(entries)
    source = dep_row.reshape(entries)
    positions = jnp.arange(entries)
    earlier = (owner_ids[:, None] == owner_ids[None, :]) & (positions[None, :] < positions[:, None])
    slot_ids = jnp.sum(earlier.astype(jnp.int32), axis=1)
    band_ids = jnp.arange(band_count, dtype=jnp.int32)
    slot_range = jnp.arange(capacity, dtype=jnp.int32)
    matches = (owner_ids[:, None, None] == band_ids[None, :, None]) & (
        slot_ids[:, None, None] == slot_range[None, None, :]
    )
    request = jnp.sum(jnp.where(matches, source[:, None, None], 0), axis=0)
    wanted = lax.all_to_all(request, "lat", split_axis=0, concat_axis=0, tiled=True)
    by_row = jnp.transpose(tracers, (2, 0, 1, 3))
    outgoing = by_row[wanted]
    incoming = lax.all_to_all(outgoing, "lat", split_axis=0, concat_axis=0, tiled=True)
    stacked_rows = incoming.reshape((band_count * capacity,) + incoming.shape[2:])
    picked = stacked_rows[owner_ids * capacity + slot_ids].reshape(
        (row_count, link_count) + stacked_rows.shape[1:]
    )
    summed = dep_weight[:, 0][:, None, None, None] * picked[:, 0]
    summed = summed + dep_weight[:, 1][:, None, None, None] * picked[:, 1]
    return jnp.transpose(summed, (1, 2, 0, 3))


def body(
    prognostic,
    tracers,
    zonal_courant,
    meridional_courant,
    filter_band,
    dep_owner,
    dep_row,
    dep_weight,
):
    row_count = prognostic.shape[2]
    departed = departure_terms(tracers, dep_owner, dep_row, dep_weight)
    lon_padded = padded(
        jnp.concatenate([prognostic, zonal_courant[None]], axis=0), (("lon", 3),), 1, True
    )
    zonal_flux = face_flux(lon_padded[:-1], lon_padded[-1:], 3)
    lat_padded = padded(
        jnp.concatenate([prognostic, meridional_courant[None]], axis=0), (("lat", 2),), 1, False
    )
    merid_flux = face_flux(lat_padded[:-1], lat_padded[-1:], 2)
    total_rows = row_count * lax.axis_size("lat")
    face_rows = lax.axis_index("lat") * row_count + jnp.arange(row_count + 1) - 1
    merid_flux = jnp.where(
        (face_rows == total_rows - 1)[None, None, :, None], jnp.float32(0.0), merid_flux
    )
    advected = (
        prognostic
        - (zonal_flux[..., 1:] - zonal_flux[..., :-1])
        - (merid_flux[:, :, 1:] - merid_flux[:, :, :-1])
    )
    new_prognostic = polar_filter(advected, filter_band)
    return (new_prognostic, departed)


def solution(mesh):
    return jax.shard_map(
        body,
        mesh=mesh,
        in_specs=(
            P(None, None, "lat", "lon"),
            P(None, None, "lat", "lon"),
            P(None, "lat", "lon"),
            P(None, "lat", "lon"),
            P("lat"),
            P("lat", None),
            P("lat", None),
            P("lat", None),
        ),
        out_specs=(P(None, None, "lat", "lon"), P(None, None, "lat", "lon")),
        check_vma=False,
    )
```

profile of v0, /device:TPU:0, one launch (start us, length us, event | category | flops | bytes accessed | tf_op | source)
XLA Modules:
  0.0 364.4 jit_solution(3108932577473310589)
XLA Ops:
  0.7 3.3 pad_maximum_fusion.8
  10.8 4.9 %collective-permute-start.2 = (f32[5,16,1,384]{3,1,2,0:T(8,128)}, f32[5,16,1,384]{3,1,2,0:T(8,128)}, u32[]{:S(2)}, u32[]{:S(2)}) collective-permute-start(f32[5,16,1,384]{3,1,2,0:T(8,128)} %copy.61), channel_id=1, source_target_pairs={{0,1},{1,2},{2,3},{3,4},{4,5},{5,6},{6,7},{8,9},{9,10},{10,11},{11... | collective-permute-start | bytes 368648 | tf_op jit(solution)/shard_map/ppermute | solution.py:17
  20.8 2.2 multiply_bitcast_fusion.1
  24.0 2.3 copy.60
  26.3 2.7 multiply_subtract_fusion
  32.6 2.3 fusion.4
  34.9 3.6 all-to-all-start
  41.5 5.8 %add_select_fusion = f32[24,64,1536]{2,1,0:T(8,128)} fusion(f32[64,1536]{1,0:T(8,128)S(1)} %get-tuple-element.21, f32[24,1536]{1,0:T(8,128)S(1)} %get-tuple-element.19, f32[64,1536]{1,0:T(8,128)S(1)} %get-tuple-element.20, f32[24,1536]{1,0:T(8,128)S(1)} %get-tuple-element.18, pred[1536]{0:T(1024)(128)(4,1)S(1)} %iota_compare_fusion.4), kind=kLoop, calls=%fused_computation.2 | loop fusion | flops 16515072 | bytes 10520064 | tf_op jit(solution)/shard_map/jit(_where)/select_n | solution.py:62
  47.3 19.7 %all-to-all-done = f32[4,384,384]{2,1,0:T(8,128)S(1)} async-done(((f32[4,384,384]{2,1,0:T(8,128)}), f32[4,384,384]{2,1,0:T(8,128)S(1)}, u32[]{:S(2)}, u32[]{:S(2)}) %all-to-all-start) | async-done | bytes 2359328 | tf_op jit(solution)/shard_map/all_to_all | solution.py:71
  67.0 6.9 %all-to-all-start.2 = ((s32[8,1,12]{2,1,0:T(1,128)}), s32[8,1,12]{2,1,0:T(1,128)S(1)}, u32[]{:S(2)}, u32[]{:S(2)}) async-start(s32[8,1,12]{2,1,0:T(1,128)} %copy.70), calls=%async_computation.2 | async-start | bytes 8192 | tf_op jit(solution)/shard_map/all_to_all | solution.py:100
  73.9 2.9 copy.65
  76.9 2.7 dot_general.8
  79.6 14.7 %convolution_multiply_fusion = f32[16,24,1536]{2,1,0:T(8,128)S(1)} fusion(f32[16,24,1536]{2,1,0:T(8,128)S(1)} %dot_general.8, f32[1536,1536,1]{1,0,2:T(8,128)} %bitcast.64, f32[24,1536]{1,0:T(8,128)S(1)} %fusion.18), kind=kOutput, calls=%fused_computation.13 | convolution fusion | flops 10872225792 | bytes 14303232 | tf_op jit(solution)/shard_map/dot_general | solution.py:73
  94.3 13.0 %fusion.31 = f32[384,4,384]{2,0,1:T(8,128)} fusion(f32[384,1536,1]{1,0,2:T(8,128)S(1)} %bitcast.71, f32[4,384,1536]{2,1,0:T(8,128)S(1)} %bitcast.65), kind=kOutput, calls=%fused_computation.87 | convolution fusion | flops 10871635968 | bytes 14155776 | tf_op jit(solution)/shard_map/dot_general | solution.py:79
  107.3 4.8 %all-to-all-start.1 = ((f32[384,4,384]{2,0,1:T(8,128)}), f32[384,4,384]{2,0,1:T(8,128)}, u32[]{:S(2)}, u32[]{:S(2)}) async-start(f32[384,4,384]{2,0,1:T(8,128)} %fusion.31), calls=%async_computation.1 | async-start | bytes 4718592 | tf_op jit(solution)/shard_map/all_to_all | solution.py:80
  112.1 2.1 copy.78
  114.3 4.8 %gather_fusion = f32[96,4,16,384]{3,2,1,0:T(8,128)} fusion(f32[24,4,16,384]{3,2,1,0:T(8,128)S(1)} %bitcast.66, s32[1024]{0:T(1024)S(1)} %pad_clamp_fusion.1), kind=kCustom, calls=%fused_computation | custom fusion | bytes 18874752 | tf_op jit(solution)/shard_map/gather | solution.py:102
  119.1 21.3 %all-to-all-done.1 = f32[384,4,384]{2,0,1:T(8,128)} async-done(((f32[384,4,384]{2,0,1:T(8,128)}), f32[384,4,384]{2,0,1:T(8,128)}, u32[]{:S(2)}, u32[]{:S(2)}) %all-to-all-start.1) | async-done | bytes 2359328 | tf_op jit(solution)/shard_map/all_to_all | solution.py:80
  140.4 6.1 %all-to-all-start.3 = ((f32[8,12,4,16,384]{4,3,2,1,0:T(8,128)}), f32[8,12,4,16,384]{4,3,2,1,0:T(8,128)}, u32[]{:S(2)}, u32[]{:S(2)}) async-start(f32[8,12,4,16,384]{4,3,2,1,0:T(8,128)} %bitcast.67), calls=%async_computation.3 | async-start | bytes 18874368 | tf_op jit(solution)/shard_map/all_to_all | solution.py:103
  146.8 3.3 add.134
  150.1 201.9 %all-to-all-done.3 = f32[8,12,4,16,384]{4,3,2,1,0:T(8,128)} async-done(((f32[8,12,4,16,384]{4,3,2,1,0:T(8,128)}), f32[8,12,4,16,384]{4,3,2,1,0:T(8,128)}, u32[]{:S(2)}, u32[]{:S(2)}) %all-to-all-start.3) | async-done | bytes 9437216 | tf_op jit(solution)/shard_map/all_to_all | solution.py:103
  352.0 6.7 %gather_fusion.1 = f32[48,4,16,384]{3,2,1,0:T(8,128)} fusion(f32[96,4,16,384]{3,2,1,0:T(8,128)} %bitcast.20, s32[1024]{0:T(1024)S(1)} %pad_clamp_fusion), kind=kCustom, calls=%fused_computation.1 | custom fusion | bytes 9437376 | tf_op jit(solution)/shard_map/gather | solution.py:105
  358.7 2.9 fusion.2
  361.6 2.8 copy.73
  (72 shorter events, 19.6 us)
Async XLA Ops:
  0.6 9.3 %copy-start = (f32[4,16,24,384]{3,2,1,0:T(8,128)S(1)}, f32[4,16,24,384]{3,2,1,0:T(8,128)}, u32[]{:S(2)}) copy-start(f32[4,16,24,384]{3,2,1,0:T(8,128)} %param.8) | copy-start | bytes 7077892
  0.6 9.3 %copy-start.3 = (f32[16,24,384]{2,1,0:T(8,128)S(1)}, f32[16,24,384]{2,1,0:T(8,128)}, u32[]{:S(2)}) copy-start(f32[16,24,384]{2,1,0:T(8,128)} %param.11) | copy-start | bytes 1769476
  4.0 13.7 %copy-start.5 = (s32[24,2]{0,1:T(2,128)S(1)}, s32[24,2]{0,1:T(2,128)}, u32[]{:S(2)}) copy-start(s32[24,2]{0,1:T(2,128)} %param.13) | copy-start | bytes 580
  4.0 14.1 %copy-start.11 = (s32[24]{0:T(128)S(1)}, s32[24]{0:T(128)}, u32[]{:S(2)}) copy-start(s32[24]{0:T(128)} %param.12) | copy-start | bytes 292
  4.0 14.1 %copy-start.7 = (s32[24,2]{0,1:T(2,128)S(1)}, s32[24,2]{0,1:T(2,128)}, u32[]{:S(2)}) copy-start(s32[24,2]{0,1:T(2,128)} %param.14) | copy-start | bytes 580
  5.7 13.8 %collective-permute-start = (f32[5,16,24,1]{2,1,3,0:T(8,128)S(1)}, f32[5,16,24,1]{2,1,3,0:T(8,128)}, u32[]{:S(2)}, u32[]{:S(2)}) collective-permute-start(f32[5,16,24,1]{2,1,3,0:T(8,128)S(1)} %copy.57), channel_id=1, source_target_pairs={{0,8},{8,16},{16,24},{24,0},{1,9},{9,17},{17,25},{25,1},{2,10},{10... | collective-permute-start | bytes 23048 | tf_op jit(solution)/shard_map/ppermute | solution.py:17
  7.9 16.1 %collective-permute-start.1 = (f32[5,16,24,1]{2,1,3,0:T(8,128)S(1)}, f32[5,16,24,1]{2,1,3,0:T(8,128)}, u32[]{:S(2)}, u32[]{:S(2)}) collective-permute-start(f32[5,16,24,1]{2,1,3,0:T(8,128)S(1)} %copy.59), channel_id=1, source_target_pairs={{8,0},{16,8},{24,16},{0,24},{9,1},{17,9},{25,17},{1,25},{10,2},{18... | collective-permute-start | bytes 23048 | tf_op jit(solution)/shard_map/ppermute | solution.py:18
  10.8 18.3 %collective-permute-start.2 = (f32[5,16,1,384]{3,1,2,0:T(8,128)}, f32[5,16,1,384]{3,1,2,0:T(8,128)}, u32[]{:S(2)}, u32[]{:S(2)}) collective-permute-start(f32[5,16,1,384]{3,1,2,0:T(8,128)} %copy.61), channel_id=1, source_target_pairs={{0,1},{1,2},{2,3},{3,4},{4,5},{5,6},{6,7},{8,9},{9,10},{10,11},{11... | collective-permute-start | bytes 368648 | tf_op jit(solution)/shard_map/ppermute | solution.py:17
  16.3 14.1 %collective-permute-start.3 = (f32[5,16,1,384]{3,1,2,0:T(8,128)}, f32[5,16,1,384]{3,1,2,0:T(8,128)}, u32[]{:S(2)}, u32[]{:S(2)}) collective-permute-start(f32[5,16,1,384]{3,1,2,0:T(8,128)} %copy.63), channel_id=1, source_target_pairs={{1,0},{2,1},{3,2},{4,3},{5,4},{6,5},{7,6},{9,8},{10,9},{11,10},{12... | collective-permute-start | bytes 368648 | tf_op jit(solution)/shard_map/ppermute | solution.py:18
  18.0 0.6 copy-start.9
  26.3 3.8 %copy-start.4 = (f32[16,24,384]{2,1,0:T(8,128)S(1)}, f32[16,24,384]{2,1,0:T(8,128)}, u32[]{:S(2)}) copy-start(f32[16,24,384]{2,1,0:T(8,128)} %param.11) | copy-start | bytes 1769476
  30.1 1.3 copy-start.8
  34.9 32.1 %all-to-all-start = ((f32[4,384,384]{2,1,0:T(8,128)}), f32[4,384,384]{2,1,0:T(8,128)S(1)}, u32[]{:S(2)}, u32[]{:S(2)}) async-start(f32[4,384,384]{2,1,0:T(8,128)} %bitcast.68), calls=%async_computation | async-start | bytes 4718592 | tf_op jit(solution)/shard_map/all_to_all | solution.py:71
  67.0 40.3 %all-to-all-start.2 = ((s32[8,1,12]{2,1,0:T(1,128)}), s32[8,1,12]{2,1,0:T(1,128)S(1)}, u32[]{:S(2)}, u32[]{:S(2)}) async-start(s32[8,1,12]{2,1,0:T(1,128)} %copy.70), calls=%async_computation.2 | async-start | bytes 8192 | tf_op jit(solution)/shard_map/all_to_all | solution.py:100
  79.6 14.8 %copy-start.1 = (f32[24,64,1536]{2,1,0:T(8,128)S(1)}, f32[24,64,1536]{2,1,0:T(8,128)}, u32[]{:S(2)}) copy-start(f32[24,64,1536]{2,1,0:T(8,128)} %add_select_fusion) | copy-start | bytes 28311556
  107.3 33.1 %all-to-all-start.1 = ((f32[384,4,384]{2,0,1:T(8,128)}), f32[384,4,384]{2,0,1:T(8,128)}, u32[]{:S(2)}, u32[]{:S(2)}) async-start(f32[384,4,384]{2,0,1:T(8,128)} %fusion.31), calls=%async_computation.1 | async-start | bytes 4718592 | tf_op jit(solution)/shard_map/all_to_all | solution.py:80
  140.4 6.3 %copy-start.10 = (s32[48]{0:T(128)S(1)}, s32[48]{0:T(128)}, u32[]{:S(2)}) copy-start(s32[48]{0:T(128)} %copy-done.9) | copy-start | bytes 580
  140.4 6.4 %copy-start.6 = (f32[24,2]{0,1:T(2,128)S(1)}, f32[24,2]{0,1:T(2,128)}, u32[]{:S(2)}) copy-start(f32[24,2]{0,1:T(2,128)} %param.15) | copy-start | bytes 580
  140.4 6.4 %copy-start.2 = (f32[4,16,24,384]{3,2,1,0:T(8,128)S(1)}, f32[4,16,24,384]{3,2,1,0:T(8,128)}, u32[]{:S(2)}) copy-start(f32[4,16,24,384]{3,2,1,0:T(8,128)} %fusion.4) | copy-start | bytes 7077892
  140.4 211.6 %all-to-all-start.3 = ((f32[8,12,4,16,384]{4,3,2,1,0:T(8,128)}), f32[8,12,4,16,384]{4,3,2,1,0:T(8,128)}, u32[]{:S(2)}, u32[]{:S(2)}) async-start(f32[8,12,4,16,384]{4,3,2,1,0:T(8,128)} %bitcast.67), calls=%async_computation.3 | async-start | bytes 18874368 | tf_op jit(solution)/shard_map/all_to_all | solution.py:103
where the time goes:
time: 365 us; the launch traced here: 364 us
  waiting for transfers between devices  243 us (67%)
  local copies, waits for them, and re-layouts  34.2 us (9%)
  starting transfers between devices  30.1 us (8%)
  other arithmetic  28.6 us (8%)
  matrix products  27.7 us (8%)
    all_to_all x1, waiting for transfers between devices, departure_terms(): lax.all_to_all(outgoing, 'lat', split_axis=0, concat_axis=0, tiled=True)  202 us
    all_to_all x1, waiting for transfers between devices, polar_filter(): lax.all_to_all(change, 'lon', split_axis=1, concat_axis=0, tiled=True)  21.3 us
    all_to_all x1, waiting for transfers between devices, polar_filter(): lax.all_to_all(flat, 'lon', split_axis=0, concat_axis=1, tiled=True)  19.7 us
    dot_general x1, matrix products, polar_filter(): spectrum = jnp.dot(circles, basis_table, precision=PRECISE)  14.7 us
    dot_general x1, matrix products, polar_filter(): lax.dot_general(scaled, basis_table, (((1,), (1,)), ((), ())), precision=...  13 us
  transfers between devices with their start and end apart: 8, of which 3 were waited for; matrix products, arithmetic and copies ran while one was open for 19% of the time, Pallas kernels for 0%

commit v1 on v0

--- a/solution.py
+++ b/solution.py
@@ -68,7 +68,16 @@
     parts = lax.axis_size("lon")
     length = block_cells * parts
     flat = values.reshape(fields * levels * rows, block_cells)
-    circles = lax.all_to_all(flat, "lon", split_axis=0, concat_axis=1, tiled=True)
+    show_racks_here = lambda page: jnp.concatenate(
+        lax.all_to_all(
+            jnp.stack(jnp.split(page, lax.axis_size("lon"), 0), 0),
+            "lon",
+            split_axis=0,
+            concat_axis=0,
+        ),
+        1,
+    )
+    circles = show_racks_here(flat)
     basis_table = circle_basis(length)
     spectrum = jnp.dot(circles, basis_table, precision=PRECISE)
     factors = column_factors(band_rows, length)

time: 365 us -> 367 us (level)
  no operation moved by 1% of the time
where the time goes in v1:
time: 367 us; the launch traced here: 366 us
  waiting for transfers between devices  243 us (66%)
  local copies, waits for them, and re-layouts  35.7 us (10%)
  starting transfers between devices  30.1 us (8%)
  other arithmetic  28.7 us (8%)
  matrix products  27.7 us (8%)
    all_to_all x1, waiting for transfers between devices, departure_terms(): lax.all_to_all(outgoing, 'lat', split_axis=0, concat_axis=0, tiled=True)  202 us
    all_to_all x1, waiting for transfers between devices, polar_filter(): lax.all_to_all(change, 'lon', split_axis=1, concat_axis=0, tiled=True)  21.3 us
    all_to_all x1, waiting for transfers between devices, polar_filter(): lax.all_to_all(jnp.stack(jnp.split(page, lax.axis_size('lon'), 0), 0), 'l...  19.7 us
    dot_general x1, matrix products, polar_filter(): spectrum = jnp.dot(circles, basis_table, precision=PRECISE)  14.7 us
    dot_general x1, matrix products, polar_filter(): lax.dot_general(scaled, basis_table, (((1,), (1,)), ((), ())), precision=...  13 us
  transfers between devices with their start and end apart: 8, of which 3 were waited for; matrix products, arithmetic and copies ran while one was open for 19% of the time, Pallas kernels for 0%

profile of v1, /device:TPU:0, one launch (start us, length us, event | category | flops | bytes accessed | tf_op | source)
XLA Modules:
  0.0 366.1 jit_solution(11269290168798170537)
XLA Ops:
  0.7 3.3 pad_maximum_fusion.9
  7.9 2.0 collective-permute-start.1
  10.7 4.9 %collective-permute-start.2 = (f32[5,16,1,384]{3,1,2,0:T(8,128)}, f32[5,16,1,384]{3,1,2,0:T(8,128)}, u32[]{:S(2)}, u32[]{:S(2)}) collective-permute-start(f32[5,16,1,384]{3,1,2,0:T(8,128)} %copy.70), channel_id=1, source_target_pairs={{0,1},{1,2},{2,3},{3,4},{4,5},{5,6},{6,7},{8,9},{9,10},{10,11},{11... | collective-permute-start | bytes 368648 | tf_op jit(solution)/shard_map/ppermute | solution.py:17
  20.8 2.2 multiply_bitcast_fusion.1
  24.0 2.3 copy.69
  26.2 2.7 multiply_subtract_fusion
  36.6 3.6 all-to-all-start
  43.2 5.8 %add_select_fusion = f32[24,64,1536]{2,1,0:T(8,128)} fusion(f32[64,1536]{1,0:T(8,128)S(1)} %get-tuple-element.25, f32[24,1536]{1,0:T(8,128)S(1)} %get-tuple-element.23, f32[64,1536]{1,0:T(8,128)S(1)} %get-tuple-element.24, f32[24,1536]{1,0:T(8,128)S(1)} %get-tuple-element.22, pred[1536]{0:T(1024)(128)(4,1)S(1)} %iota_compare_fusion.4), kind=kLoop, calls=%fused_computation.2 | loop fusion | flops 16515072 | bytes 10520064 | tf_op jit(solution)/shard_map/jit(_where)/select_n | solution.py:62
  49.0 19.7 %all-to-all-done = f32[4,384,384]{2,1,0:T(8,128)S(1)} async-done(((f32[4,384,384]{2,1,0:T(8,128)}), f32[4,384,384]{2,1,0:T(8,128)S(1)}, u32[]{:S(2)}, u32[]{:S(2)}) %all-to-all-start) | async-done | bytes 2359328 | tf_op jit(solution)/shard_map/all_to_all | solution.py:72
  68.7 6.9 %all-to-all-start.2 = ((s32[8,1,12]{2,1,0:T(1,128)}), s32[8,1,12]{2,1,0:T(1,128)S(1)}, u32[]{:S(2)}, u32[]{:S(2)}) async-start(s32[8,1,12]{2,1,0:T(1,128)} %copy.79), calls=%async_computation.2 | async-start | bytes 8192 | tf_op jit(solution)/shard_map/all_to_all | solution.py:109
  75.6 2.9 copy.74
  78.5 2.7 dot_general.8
  81.3 14.7 %convolution_multiply_fusion = f32[16,24,1536]{2,1,0:T(8,128)S(1)} fusion(f32[16,24,1536]{2,1,0:T(8,128)S(1)} %dot_general.8, f32[1536,1536,1]{1,0,2:T(8,128)} %bitcast.67, f32[24,1536]{1,0:T(8,128)S(1)} %fusion.18), kind=kOutput, calls=%fused_computation.13 | convolution fusion | flops 10872225792 | bytes 14303232 | tf_op jit(solution)/shard_map/dot_general | solution.py:82
  96.0 13.0 %fusion.32 = f32[384,4,384]{2,0,1:T(8,128)} fusion(f32[384,1536,1]{1,0,2:T(8,128)S(1)} %bitcast.73, f32[4,384,1536]{2,1,0:T(8,128)S(1)} %bitcast.68), kind=kOutput, calls=%fused_computation.89 | convolution fusion | flops 10871635968 | bytes 14155776 | tf_op jit(solution)/shard_map/dot_general | solution.py:88
  109.0 4.8 %all-to-all-start.1 = ((f32[384,4,384]{2,0,1:T(8,128)}), f32[384,4,384]{2,0,1:T(8,128)}, u32[]{:S(2)}, u32[]{:S(2)}) async-start(f32[384,4,384]{2,0,1:T(8,128)} %fusion.32), calls=%async_computation.1 | async-start | bytes 4718592 | tf_op jit(solution)/shard_map/all_to_all | solution.py:89
  113.8 2.1 copy.87
  116.0 4.8 %gather_fusion = f32[96,4,16,384]{3,2,1,0:T(8,128)} fusion(f32[24,4,16,384]{3,2,1,0:T(8,128)S(1)} %bitcast.69, s32[1024]{0:T(1024)S(1)} %pad_clamp_fusion.1), kind=kCustom, calls=%fused_computation | custom fusion | bytes 18874752 | tf_op jit(solution)/shard_map/gather | solution.py:111
  120.8 21.3 %all-to-all-done.1 = f32[384,4,384]{2,0,1:T(8,128)} async-done(((f32[384,4,384]{2,0,1:T(8,128)}), f32[384,4,384]{2,0,1:T(8,128)}, u32[]{:S(2)}, u32[]{:S(2)}) %all-to-all-start.1) | async-done | bytes 2359328 | tf_op jit(solution)/shard_map/all_to_all | solution.py:89
  142.1 6.1 %all-to-all-start.3 = ((f32[8,12,4,16,384]{4,3,2,1,0:T(8,128)}), f32[8,12,4,16,384]{4,3,2,1,0:T(8,128)}, u32[]{:S(2)}, u32[]{:S(2)}) async-start(f32[8,12,4,16,384]{4,3,2,1,0:T(8,128)} %bitcast.70), calls=%async_computation.3 | async-start | bytes 18874368 | tf_op jit(solution)/shard_map/all_to_all | solution.py:112
  148.5 3.3 add.134
  151.8 201.9 %all-to-all-done.3 = f32[8,12,4,16,384]{4,3,2,1,0:T(8,128)} async-done(((f32[8,12,4,16,384]{4,3,2,1,0:T(8,128)}), f32[8,12,4,16,384]{4,3,2,1,0:T(8,128)}, u32[]{:S(2)}, u32[]{:S(2)}) %all-to-all-start.3) | async-done | bytes 9437216 | tf_op jit(solution)/shard_map/all_to_all | solution.py:112
  353.7 6.8 %gather_fusion.1 = f32[48,4,16,384]{3,2,1,0:T(8,128)} fusion(f32[96,4,16,384]{3,2,1,0:T(8,128)} %bitcast.23, s32[1024]{0:T(1024)S(1)} %pad_clamp_fusion), kind=kCustom, calls=%fused_computation.1 | custom fusion | bytes 9437376 | tf_op jit(solution)/shard_map/gather | solution.py:114
  360.4 2.9 fusion.2
  363.3 2.8 copy.82
  (76 shorter events, 21.6 us)
Async XLA Ops:
  0.6 9.3 %copy-start = (f32[4,16,24,384]{3,2,1,0:T(8,128)S(1)}, f32[4,16,24,384]{3,2,1,0:T(8,128)}, u32[]{:S(2)}) copy-start(f32[4,16,24,384]{3,2,1,0:T(8,128)} %param.8) | copy-start | bytes 7077892
  0.6 9.3 %copy-start.4 = (f32[16,24,384]{2,1,0:T(8,128)S(1)}, f32[16,24,384]{2,1,0:T(8,128)}, u32[]{:S(2)}) copy-start(f32[16,24,384]{2,1,0:T(8,128)} %param.11) | copy-start | bytes 1769476
  4.0 13.6 %copy-start.6 = (s32[24,2]{0,1:T(2,128)S(1)}, s32[24,2]{0,1:T(2,128)}, u32[]{:S(2)}) copy-start(s32[24,2]{0,1:T(2,128)} %param.13) | copy-start | bytes 580
  4.0 14.0 %copy-start.12 = (s32[24]{0:T(128)S(1)}, s32[24]{0:T(128)}, u32[]{:S(2)}) copy-start(s32[24]{0:T(128)} %param.12) | copy-start | bytes 292
  4.0 14.1 %copy-start.8 = (s32[24,2]{0,1:T(2,128)S(1)}, s32[24,2]{0,1:T(2,128)}, u32[]{:S(2)}) copy-start(s32[24,2]{0,1:T(2,128)} %param.14) | copy-start | bytes 580
  5.7 13.8 %collective-permute-start = (f32[5,16,24,1]{2,1,3,0:T(8,128)S(1)}, f32[5,16,24,1]{2,1,3,0:T(8,128)}, u32[]{:S(2)}, u32[]{:S(2)}) collective-permute-start(f32[5,16,24,1]{2,1,3,0:T(8,128)S(1)} %copy.66), channel_id=1, source_target_pairs={{0,8},{8,16},{16,24},{24,0},{1,9},{9,17},{17,25},{25,1},{2,10},{10... | collective-permute-start | bytes 23048 | tf_op jit(solution)/shard_map/ppermute | solution.py:17
  7.9 16.1 %collective-permute-start.1 = (f32[5,16,24,1]{2,1,3,0:T(8,128)S(1)}, f32[5,16,24,1]{2,1,3,0:T(8,128)}, u32[]{:S(2)}, u32[]{:S(2)}) collective-permute-start(f32[5,16,24,1]{2,1,3,0:T(8,128)S(1)} %copy.68), channel_id=1, source_target_pairs={{8,0},{16,8},{24,16},{0,24},{9,1},{17,9},{25,17},{1,25},{10,2},{18... | collective-permute-start | bytes 23048 | tf_op jit(solution)/shard_map/ppermute | solution.py:18
  10.7 18.3 %collective-permute-start.2 = (f32[5,16,1,384]{3,1,2,0:T(8,128)}, f32[5,16,1,384]{3,1,2,0:T(8,128)}, u32[]{:S(2)}, u32[]{:S(2)}) collective-permute-start(f32[5,16,1,384]{3,1,2,0:T(8,128)} %copy.70), channel_id=1, source_target_pairs={{0,1},{1,2},{2,3},{3,4},{4,5},{5,6},{6,7},{8,9},{9,10},{10,11},{11... | collective-permute-start | bytes 368648 | tf_op jit(solution)/shard_map/ppermute | solution.py:17
  16.2 14.1 %collective-permute-start.3 = (f32[5,16,1,384]{3,1,2,0:T(8,128)}, f32[5,16,1,384]{3,1,2,0:T(8,128)}, u32[]{:S(2)}, u32[]{:S(2)}) collective-permute-start(f32[5,16,1,384]{3,1,2,0:T(8,128)} %copy.72), channel_id=1, source_target_pairs={{1,0},{2,1},{3,2},{4,3},{5,4},{6,5},{7,6},{9,8},{10,9},{11,10},{12... | collective-permute-start | bytes 368648 | tf_op jit(solution)/shard_map/ppermute | solution.py:18
  18.0 0.6 copy-start.10
  26.2 3.8 %copy-start.5 = (f32[16,24,384]{2,1,0:T(8,128)S(1)}, f32[16,24,384]{2,1,0:T(8,128)}, u32[]{:S(2)}) copy-start(f32[16,24,384]{2,1,0:T(8,128)} %param.11) | copy-start | bytes 1769476
  30.1 1.3 copy-start.9
  33.4 1.4 copy-start.2
  36.6 32.1 %all-to-all-start = ((f32[4,384,384]{2,1,0:T(8,128)}), f32[4,384,384]{2,1,0:T(8,128)S(1)}, u32[]{:S(2)}, u32[]{:S(2)}) async-start(f32[4,384,384]{2,1,0:T(8,128)} %pad_maximum_fusion.8), calls=%async_computation | async-start | bytes 4718592 | tf_op jit(solution)/shard_map/all_to_all | solution.py:72
  68.7 40.3 %all-to-all-start.2 = ((s32[8,1,12]{2,1,0:T(1,128)}), s32[8,1,12]{2,1,0:T(1,128)S(1)}, u32[]{:S(2)}, u32[]{:S(2)}) async-start(s32[8,1,12]{2,1,0:T(1,128)} %copy.79), calls=%async_computation.2 | async-start | bytes 8192 | tf_op jit(solution)/shard_map/all_to_all | solution.py:109
  81.3 14.8 %copy-start.1 = (f32[24,64,1536]{2,1,0:T(8,128)S(1)}, f32[24,64,1536]{2,1,0:T(8,128)}, u32[]{:S(2)}) copy-start(f32[24,64,1536]{2,1,0:T(8,128)} %add_select_fusion) | copy-start | bytes 28311556
  109.0 33.1 %all-to-all-start.1 = ((f32[384,4,384]{2,0,1:T(8,128)}), f32[384,4,384]{2,0,1:T(8,128)}, u32[]{:S(2)}, u32[]{:S(2)}) async-start(f32[384,4,384]{2,0,1:T(8,128)} %fusion.32), calls=%async_computation.1 | async-start | bytes 4718592 | tf_op jit(solution)/shard_map/all_to_all | solution.py:89
  142.1 6.3 %copy-start.11 = (s32[48]{0:T(128)S(1)}, s32[48]{0:T(128)}, u32[]{:S(2)}) copy-start(s32[48]{0:T(128)} %copy-done.10) | copy-start | bytes 580
  142.1 6.4 %copy-start.7 = (f32[24,2]{0,1:T(2,128)S(1)}, f32[24,2]{0,1:T(2,128)}, u32[]{:S(2)}) copy-start(f32[24,2]{0,1:T(2,128)} %param.15) | copy-start | bytes 580
  142.1 6.4 %copy-start.3 = (f32[4,16,24,384]{3,2,1,0:T(8,128)S(1)}, f32[4,16,24,384]{3,2,1,0:T(8,128)}, u32[]{:S(2)}) copy-start(f32[4,16,24,384]{3,2,1,0:T(8,128)} %copy-done.2) | copy-start | bytes 7077892
  142.1 211.6 %all-to-all-start.3 = ((f32[8,12,4,16,384]{4,3,2,1,0:T(8,128)}), f32[8,12,4,16,384]{4,3,2,1,0:T(8,128)}, u32[]{:S(2)}, u32[]{:S(2)}) async-start(f32[8,12,4,16,384]{4,3,2,1,0:T(8,128)} %bitcast.70), calls=%async_computation.3 | async-start | bytes 18874368 | tf_op jit(solution)/shard_map/all_to_all | solution.py:112
